TPU v7x, 32 devices: a whole 2x2x4 slice. The times are simulated.
32 devices in a mesh: narrow: 8 (over z, x), wide: 4 (over y, core).
Axes of the slice: x: 2, y: 2, z: 4, core: 2. Of those that a mesh axis runs over, the one named last changes fastest.
Arguments:
- amps: bfloat16 [16, 512, 512], P(None, 'narrow', 'wide'), may hold values from -1 to 1
- left_fit: bfloat16 [64, 512, 256], P(None, 'narrow'), may hold values from -0.375 to 0.375
- right_fit: bfloat16 [512, 512, 256], P('narrow', 'wide'), may hold values from -0.375 to 0.375
- pair_list: int32 [16, 2], P('narrow'), may hold values from 0 to 127, as said below
- occ_energy: float32 [128], replicated, may hold values from -2 to -0.5
- vir_energy: float32 [512], replicated, may hold values from 0.5 to 3
Outputs:
- update: float32 [16, 64, 512], P('narrow', None, 'wide')
Inputs may be any that keep to these rules, and one draw needn't show every extreme that they name: `pair_list`: each row (i, j) has i <= j.
All inputs are finite; a program needn't handle non-finite values.
Results may differ from a plain program's by a relative error of at most 0.0029.
Values may be sent and summed in bfloat16 or wider, within the bound.
No kernel may reach another device: no remote copies, remote signals or barrier semaphores. Data moves between devices by JAX's collectives and lax.ppermute only.
A program may use at most 128 MiB of HBM per device.

v0:
```python
import jax
import jax.numpy as jnp
from jax import lax
from jax.sharding import PartitionSpec as P


def body(amps, left_fit, right_fit, pair_list, occ_energy, vir_energy):
    right_all = lax.all_gather(right_fit, "narrow", axis=0, tiled=True)
    vir_total, col_width, aux_width = right_all.shape
    right_mat = right_all.reshape(vir_total, col_width * aux_width)
    rows_total = left_fit.shape[0]
    amps_full = lax.all_to_all(amps, "narrow", split_axis=0, concat_axis=1, tiled=True)
    pairs_here = amps_full.shape[0]
    partials = []
    for start_row in range(0, rows_total, 16):
        row_block = left_fit[start_row : start_row + 16]
        running = jnp.einsum(
            "acq,pcd->padq",
            lax.all_gather(row_block, "narrow", axis=1, tiled=True),
            amps_full,
            preferred_element_type=jnp.float32,
        )
        rows_here = running.shape[1]
        mixed_rows = running.astype(jnp.bfloat16).reshape(
            pairs_here * rows_here, col_width * aux_width
        )
        project_ladder_part = lax.dot_general(
            mixed_rows, right_mat, (((1,), (1,)), ((), ())), preferred_element_type=jnp.float32
        )
        partials.append(project_ladder_part.reshape(pairs_here, rows_here, vir_total))
    reduced = [
        lax.psum_scatter(ladder_part, "wide", scatter_dimension=2, tiled=True)
        for ladder_part in partials
    ]
    ladder_sum = jnp.concatenate(reduced, axis=1)
    local_cols = ladder_sum.shape[2]
    occ_ids = jnp.arange(occ_energy.shape[0], dtype=jnp.int32)
    occ_first = jnp.sum(
        jnp.where(pair_list[:, 0:1] == occ_ids[None, :], occ_energy[None, :], 0.0), axis=1
    )
    occ_second = jnp.sum(
        jnp.where(pair_list[:, 1:2] == occ_ids[None, :], occ_energy[None, :], 0.0), axis=1
    )
    vir_cols = lax.dynamic_slice_in_dim(
        vir_energy, lax.axis_index("wide") * local_cols, local_cols, 0
    )
    vir_rows = vir_energy[:rows_total]
    denominator = (
        (occ_first + occ_second)[:, None, None] - vir_rows[None, :, None] - vir_cols[None, None, :]
    )
    return ladder_sum / denominator


def solution(mesh):
    return jax.shard_map(
        body,
        mesh=mesh,
        in_specs=(
            P(None, "narrow", "wide"),
            P(None, "narrow", None),
            P("narrow", "wide", None),
            P("narrow", None),
            P(),
            P(),
        ),
        out_specs=P("narrow", None, "wide"),
        check_vma=False,
    )
```

profile of v0, /device:TPU:0, one launch (start us, length us, event | category | flops | bytes accessed | tf_op | source)
XLA Modules:
  0.0 1060.1 jit_solution(1422802223781420822)
XLA Ops:
  6.5 0.0 all-gather.14.cloned.1.call-start
  6.5 2.9 fusion.50
  9.4 0.0 all-gather.14.cloned.1.call-update
  9.5 0.0 all-gather.12.cloned.1.call-start
  9.5 0.7 all-gather.12.cloned.1.call-update
  10.2 0.0 all-gather.10.cloned.1.call-start
  10.3 0.7 all-gather.10.cloned.1.call-update
  11.0 0.0 all-gather.6.cloned.1.call-start
  11.0 0.5 all-gather.6.cloned.1.call-update
  11.5 0.0 all-gather.8.cloned.1.call-start
  11.6 6.5 copy.21
  18.1 0.0 copy-start.2
  18.1 0.0 all-gather.8.cloned.1.call-update
  18.1 7.4 all-to-all-start
  25.5 0.0 reduce-scatter.11.cloned.1.call-start
  25.6 0.0 copy-done.2
  25.6 0.1 dynamic_slice.3
  25.7 0.0 copy-done
  25.7 0.2 slice_reduce_fusion
  25.8 0.0 copy-done.1
  25.8 0.2 fusion.49
  26.1 16.1 %all-to-all-done = bf16[16,64,128]{2,1,0:T(8,128)(2,1)S(1)} async-done(((bf16[16,64,128]{2,1,0:T(8,128)(2,1)}), bf16[16,64,128]{2,1,0:T(8,128)(2,1)S(1)}, u32[]{:S(2)}, u32[]{:S(2)}) %all-to-all-start) | async-done | bytes 262176 | tf_op jit(solution)/shard_map/all_to_all | solution.py:12
  42.2 49.1 %all-gather.14.cloned.1.call-done = bf16[16,512,256]{2,1,0:T(8,128)(2,1)} async-done(((bf16[16,64,256]{2,1,0:T(8,128)(2,1)}), bf16[16,512,256]{2,1,0:T(8,128)(2,1)}) %all-gather.14.cloned.1.call-update) | async-done | bytes 4194320 | tf_op jit(solution)/shard_map/all_gather | solution.py:19
  91.2 4.8 convert_bitcast_fusion
  96.0 69.1 %all-gather.12.cloned.1.call-done = bf16[16,512,256]{2,1,0:T(8,128)(2,1)} async-done(((bf16[16,64,256]{2,1,0:T(8,128)(2,1)}), bf16[16,512,256]{2,1,0:T(8,128)(2,1)}) %all-gather.12.cloned.1.call-update) | async-done | bytes 4194320 | tf_op jit(solution)/shard_map/all_gather | solution.py:19
  165.1 4.8 convert_bitcast_fusion.1
  169.9 69.1 %all-gather.10.cloned.1.call-done = bf16[16,512,256]{2,1,0:T(8,128)(2,1)} async-done(((bf16[16,64,256]{2,1,0:T(8,128)(2,1)}), bf16[16,512,256]{2,1,0:T(8,128)(2,1)}) %all-gather.10.cloned.1.call-update) | async-done | bytes 4194320 | tf_op jit(solution)/shard_map/all_gather | solution.py:19
  239.0 4.9 convert_bitcast_fusion.2
  243.8 68.9 %all-gather.6.cloned.1.call-done = bf16[16,512,256]{2,1,0:T(8,128)(2,1)} async-done(((bf16[16,64,256]{2,1,0:T(8,128)(2,1)}), bf16[16,512,256]{2,1,0:T(8,128)(2,1)}) %all-gather.6.cloned.1.call-update) | async-done | bytes 4194320 | tf_op jit(solution)/shard_map/all_gather | solution.py:19
  312.7 3.5 convert_bitcast_fusion.3
  316.2 634.0 %all-gather.8.cloned.1.call-done = bf16[512,128,256]{2,0,1:T(8,128)(2,1)} async-done(((bf16[64,128,256]{2,0,1:T(8,128)(2,1)}), bf16[512,128,256]{2,0,1:T(8,128)(2,1)}) %all-gather.8.cloned.1.call-update) | async-done | bytes 33554448 | tf_op jit(solution)/shard_map/all_gather | solution.py:8
  950.1 16.3 %fusion.43 = f32[2,16,512]{2,1,0:T(8,128)} fusion(bf16[512,128,256]{2,0,1:T(8,128)(2,1)} %all-gather.8.cloned.1.call-done, bf16[2,16,128,256]{3,2,1,0:T(8,128)(2,1)} %convert_bitcast_fusion), kind=kOutput, calls=%fused_computation.27 | convolution fusion | flops 1073741824 | bytes 35717120 | tf_op jit(solution)/shard_map/dot_general | solution.py:27
  966.4 0.0 reduce-scatter.11.cloned.1.call-update
  966.4 0.0 reduce-scatter.9.cloned.1.call-start
  966.5 16.3 %fusion.38 = f32[2,16,512]{2,1,0:T(8,128)} fusion(bf16[512,128,256]{2,0,1:T(8,128)(2,1)} %all-gather.8.cloned.1.call-done, bf16[2,16,128,256]{3,2,1,0:T(8,128)(2,1)} %convert_bitcast_fusion.1), kind=kOutput, calls=%fused_computation.26 | convolution fusion | flops 1073741824 | bytes 35717120 | tf_op jit(solution)/shard_map/dot_general | solution.py:27
  982.8 0.0 reduce-scatter.9.cloned.1.call-update
  982.8 0.2 reduce-scatter.7.cloned.1.call-start
  983.0 16.3 %fusion.33 = f32[2,16,512]{2,1,0:T(8,128)} fusion(bf16[512,128,256]{2,0,1:T(8,128)(2,1)} %all-gather.8.cloned.1.call-done, bf16[2,16,128,256]{3,2,1,0:T(8,128)(2,1)} %convert_bitcast_fusion.2), kind=kOutput, calls=%fused_computation.25 | convolution fusion | flops 1073741824 | bytes 35717120 | tf_op jit(solution)/shard_map/dot_general | solution.py:27
  999.4 0.0 reduce-scatter.7.cloned.1.call-update
  999.4 0.0 slice-start
  999.4 0.0 reduce-scatter.5.cloned.1.call-start
  999.4 15.9 %fusion.28 = f32[2,16,512]{2,1,0:T(8,128)} fusion(bf16[512,128,256]{2,0,1:T(8,128)(2,1)} %all-gather.8.cloned.1.call-done, bf16[2,16,128,256]{3,2,1,0:T(8,128)(2,1)S(1)} %convert_bitcast_fusion.3), kind=kOutput, calls=%fused_computation.24 | convolution fusion | flops 1073741824 | bytes 35717120 | tf_op jit(solution)/shard_map/dot_general | solution.py:27
  1015.3 0.0 reduce-scatter.5.cloned.1.call-update
  1015.4 0.0 slice-done
  1015.4 0.1 broadcast_subtract_fusion
  1015.5 14.6 %reduce-scatter.7.cloned.1.call-done = f32[2,16,128]{2,1,0:T(8,128)} async-done(((f32[2,16,512]{2,1,0:T(8,128)}), f32[2,16,128]{2,1,0:T(8,128)}) %reduce-scatter.7.cloned.1.call-update) | async-done | bytes 16400 | tf_op jit(solution)/shard_map/reduce_scatter | solution.py:32
  1030.0 22.0 %reduce-scatter.5.cloned.1.call-done = f32[2,16,128]{2,1,0:T(8,128)} async-done(((f32[2,16,512]{2,1,0:T(8,128)}), f32[2,16,128]{2,1,0:T(8,128)}) %reduce-scatter.5.cloned.1.call-update) | async-done | bytes 16400 | tf_op jit(solution)/shard_map/reduce_scatter | solution.py:32
  1052.1 1.5 maximum_divide_fusion
  (6 shorter events, 0.0 us)
Async XLA Ops:
  6.5 84.7 %all-gather.14.cloned.1.call-start = ((), (), s32[]{:S(2)}) async-start(), calls=%async_computation.12 | async-start | bytes 4718592 | tf_op jit(solution)/shard_map/all_gather | solution.py:19
  9.5 155.6 %all-gather.12.cloned.1.call-start = ((), (), s32[]{:S(2)}) async-start(), calls=%async_computation.10 | async-start | bytes 4718592 | tf_op jit(solution)/shard_map/all_gather | solution.py:19
  10.2 228.8 %all-gather.10.cloned.1.call-start = ((), (), s32[]{:S(2)}) async-start(), calls=%async_computation.8 | async-start | bytes 4718592 | tf_op jit(solution)/shard_map/all_gather | solution.py:19
  11.0 301.7 %all-gather.6.cloned.1.call-start = ((), (), s32[]{:S(2)}) async-start(), calls=%async_computation.5 | async-start | bytes 4718592 | tf_op jit(solution)/shard_map/all_gather | solution.py:19
  11.5 938.6 %all-gather.8.cloned.1.call-start = ((), (), s32[]{:S(2)}) async-start(), calls=%async_computation.6 | async-start | bytes 37748736 | tf_op jit(solution)/shard_map/all_gather | solution.py:8
  18.1 7.5 copy-start.2
  18.1 7.6 copy-start
  18.1 7.7 copy-start.1
  18.1 24.0 %all-to-all-start = ((bf16[16,64,128]{2,1,0:T(8,128)(2,1)}), bf16[16,64,128]{2,1,0:T(8,128)(2,1)S(1)}, u32[]{:S(2)}, u32[]{:S(2)}) async-start(bf16[16,64,128]{2,1,0:T(8,128)(2,1)} %param.6), calls=%async_computation | async-start | bytes 524288 | tf_op jit(solution)/shard_map/all_to_all | solution.py:12
  25.5 989.9 %reduce-scatter.11.cloned.1.call-start = ((), (), s32[]{:S(2)}) async-start(), calls=%async_computation.13 | async-start | bytes 81920 | tf_op jit(solution)/shard_map/reduce_scatter | solution.py:32
  966.4 49.0 %reduce-scatter.9.cloned.1.call-start = ((), (), s32[]{:S(2)}) async-start(), calls=%async_computation.11 | async-start | bytes 81920 | tf_op jit(solution)/shard_map/reduce_scatter | solution.py:32
  982.8 47.2 %reduce-scatter.7.cloned.1.call-start = ((), (), s32[]{:S(2)}) async-start(), calls=%async_computation.9 | async-start | bytes 81920 | tf_op jit(solution)/shard_map/reduce_scatter | solution.py:32
  999.4 16.0 %slice-start = ((f32[512]{0:T(512)}), f32[64]{0:T(128)S(1)}, s32[]{:S(2)}) async-start(f32[512]{0:T(512)} %param.11), calls=%async_computation.14 | async-start | bytes 1024 | tf_op jit(solution)/shard_map/slice | solution.py:47
  999.4 52.7 %reduce-scatter.5.cloned.1.call-start = ((), (), s32[]{:S(2)}) async-start(), calls=%async_computation.7 | async-start | bytes 81920 | tf_op jit(solution)/shard_map/reduce_scatter | solution.py:32
Sparse Core Ops, SparseCore 0:
  9.6 81.6 all-gather.13
  93.4 71.6 all-gather.11
  167.3 71.6 all-gather.9
  241.0 71.6 all-gather.5
  314.1 635.9 all-gather.7
  966.5 19.4 reduce-scatter.10
  988.6 19.4 reduce-scatter.8
  1010.5 19.5 reduce-scatter.6
  1032.6 19.4 reduce-scatter.4
where the time goes:
time: 1060 us
  waiting for transfers between devices  945 us (89%)
  matrix products  82.7 us (8%)
  between operations  13.3 us (1%)
    all_gather x1, waiting for transfers between devices, body(): right_all = lax.all_gather(right_fit, 'narrow', axis=0, tiled=True)  634 us
    all_gather x4, waiting for transfers between devices, body(): lax.all_gather(row_block, 'narrow', axis=1, tiled=True)  256 us
    dot_general x4, matrix products, body(): lax.dot_general(mixed_rows, right_mat, (((1,), (1,)), ((), ())), preferre...  64.8 us
    reduce_scatter x4, waiting for transfers between devices, body(): lax.psum_scatter(ladder_part, 'wide', scatter_dimension=2, tiled=True)  36.6 us
  transfers between devices with their start and end apart: 10, of which 8 were waited for; matrix products, arithmetic and copies ran while one was open for 7% of the time, Pallas kernels for 0%

commit v1 on v0

--- a/solution.py
+++ b/solution.py
@@ -5,7 +5,14 @@
 
 
 def body(amps, left_fit, right_fit, pair_list, occ_energy, vir_energy):
-    right_all = lax.all_gather(right_fit, "narrow", axis=0, tiled=True)
+    ring = [right_fit]
+    for hop in range(7):
+        ring.append(lax.ppermute(ring[-1], "narrow", [(dev, (dev + 1) % 8) for dev in range(8)]))
+    right_all = jnp.roll(
+        jnp.concatenate(ring[::-1], axis=0),
+        (lax.axis_index("narrow") + 1) * ring[0].shape[0],
+        axis=0,
+    )
     vir_total, col_width, aux_width = right_all.shape
     right_mat = right_all.reshape(vir_total, col_width * aux_width)
     rows_total = left_fit.shape[0]

time: 1060 us -> 1070 us (level)
  local copies, waits for them, and re-layouts: 9.72 us -> 82.8 us
  waiting for transfers between devices: 945 us -> 883 us
    ppermute x0 -> x7, waiting for transfers between devices: none -> 761 us  [body(): lax.ppermute(ring[-1], 'narrow', [(dev, (dev + 1) % 8) for dev in range(8)])]
    all_gather x1 -> x0, waiting for transfers between devices: 634 us -> none  [body(): right_all = lax.all_gather(right_fit, 'narrow', axis=0, tiled=True)]
    all_gather x4, waiting for transfers between devices: 256 us -> 0.03 us  [body(): lax.all_gather(row_block, 'narrow', axis=1, tiled=True)]
    all_to_all x1, waiting for transfers between devices: 16.1 us -> 87.2 us  [body(): lax.all_to_all(amps, 'narrow', split_axis=0, concat_axis=1, tiled=True)]
    unnamed x7 -> x26, local copies, waits for them, and re-layouts: 6.52 us -> 74.9 us
  transfers between devices with their start and end apart: 10 -> 16, of which waited for: 8 -> 9; matrix products, arithmetic and copies ran while one was open for 7% -> 7% of each run, Pallas kernels for 0% -> 0%
where the time goes in v1:
time: 1070 us
  waiting for transfers between devices  883 us (83%)
  local copies, waits for them, and re-layouts  82.8 us (8%)
  matrix products  82.4 us (8%)
  between operations  13.6 us (1%)
    ppermute x7, waiting for transfers between devices, body(): lax.ppermute(ring[-1], 'narrow', [(dev, (dev + 1) % 8) for dev in range(8)])  761 us
    all_to_all x1, waiting for transfers between devices, body(): lax.all_to_all(amps, 'narrow', split_axis=0, concat_axis=1, tiled=True)  87.2 us
    unnamed x26, local copies, waits for them, and re-layouts  74.9 us
    dot_general x4, matrix products, body(): lax.dot_general(mixed_rows, right_mat, (((1,), (1,)), ((), ())), preferre...  64.5 us
    reduce_scatter x4, waiting for transfers between devices, body(): lax.psum_scatter(ladder_part, 'wide', scatter_dimension=2, tiled=True)  34.7 us
  transfers between devices with their start and end apart: 16, of which 9 were waited for; matrix products, arithmetic and copies ran while one was open for 7% of the time, Pallas kernels for 0%

profile of v1, /device:TPU:0, one launch (start us, length us, event | category | flops | bytes accessed | tf_op | source)
XLA Modules:
  0.0 1072.8 jit_solution(2306669467824012857)
XLA Ops:
  6.5 2.9 fusion.58
  9.6 4.6 copy.27
  14.1 3.0 collective-permute-start
  17.1 144.4 %collective-permute-done = bf16[64,128,256]{2,0,1:T(8,128)(2,1)} collective-permute-done((bf16[64,128,256]{2,0,1:T(8,128)(2,1)S(1)}, bf16[64,128,256]{2,0,1:T(8,128)(2,1)}, u32[]{:S(2)}, u32[]{:S(2)}) %collective-permute-start) | collective-permute-done | bytes 4194336 | tf_op jit(solution)/shard_map/ppermute | solution.py:10
  161.5 0.0 all-gather.7.cloned.1.call-start
  161.6 145.3 %collective-permute-done.1 = bf16[64,128,256]{2,0,1:T(8,128)(2,1)} collective-permute-done((bf16[64,128,256]{2,0,1:T(8,128)(2,1)}, bf16[64,128,256]{2,0,1:T(8,128)(2,1)}, u32[]{:S(2)}, u32[]{:S(2)}) %collective-permute-start.1) | collective-permute-done | bytes 4194336 | tf_op jit(solution)/shard_map/ppermute | solution.py:10
  306.9 93.8 %collective-permute-done.2 = bf16[64,128,256]{2,0,1:T(8,128)(2,1)} collective-permute-done((bf16[64,128,256]{2,0,1:T(8,128)(2,1)}, bf16[64,128,256]{2,0,1:T(8,128)(2,1)}, u32[]{:S(2)}, u32[]{:S(2)}) %collective-permute-start.2) | collective-permute-done | bytes 4194336 | tf_op jit(solution)/shard_map/ppermute | solution.py:10
  400.8 0.0 all-gather.5.cloned.1.call-start
  400.8 143.5 %collective-permute-done.3 = bf16[64,128,256]{2,0,1:T(8,128)(2,1)} collective-permute-done((bf16[64,128,256]{2,0,1:T(8,128)(2,1)}, bf16[64,128,256]{2,0,1:T(8,128)(2,1)}, u32[]{:S(2)}, u32[]{:S(2)}) %collective-permute-start.3) | collective-permute-done | bytes 4194336 | tf_op jit(solution)/shard_map/ppermute | solution.py:10
  544.3 92.0 %collective-permute-done.4 = bf16[64,128,256]{2,0,1:T(8,128)(2,1)} collective-permute-done((bf16[64,128,256]{2,0,1:T(8,128)(2,1)}, bf16[64,128,256]{2,0,1:T(8,128)(2,1)}, u32[]{:S(2)}, u32[]{:S(2)}) %collective-permute-start.4) | collective-permute-done | bytes 4194336 | tf_op jit(solution)/shard_map/ppermute | solution.py:10
  636.3 141.7 %collective-permute-done.5 = bf16[64,128,256]{2,0,1:T(8,128)(2,1)} collective-permute-done((bf16[64,128,256]{2,0,1:T(8,128)(2,1)}, bf16[64,128,256]{2,0,1:T(8,128)(2,1)}, u32[]{:S(2)}, u32[]{:S(2)}) %collective-permute-start.5) | collective-permute-done | bytes 4194336 | tf_op jit(solution)/shard_map/ppermute | solution.py:10
  778.1 6.0 all-to-all-start
  784.0 0.2 reduce-scatter.11.cloned.1.call-start
  784.3 0.1 dynamic_slice.8
  784.4 0.2 slice_reduce_fusion
  784.6 0.2 fusion.53
  784.8 87.2 %all-to-all-done = bf16[16,64,128]{2,1,0:T(8,128)(2,1)S(1)} async-done(((bf16[16,64,128]{2,1,0:T(8,128)(2,1)}), bf16[16,64,128]{2,1,0:T(8,128)(2,1)S(1)}, u32[]{:S(2)}, u32[]{:S(2)}) %all-to-all-start) | async-done | bytes 262176 | tf_op jit(solution)/shard_map/all_to_all | solution.py:19
  872.0 4.9 convert_bitcast_fusion
  876.9 4.8 convert_bitcast_fusion.1
  881.7 4.8 convert_bitcast_fusion.2
  886.4 3.5 convert_bitcast_fusion.3
  889.9 4.7 constant_dynamic-update-slice_fusion.15
  894.6 4.7 constant_dynamic-update-slice_fusion.14
  899.3 4.7 constant_dynamic-update-slice_fusion.13
  904.0 4.8 constant_dynamic-update-slice_fusion.12
  908.7 4.7 constant_dynamic-update-slice_fusion.11
  913.4 4.6 constant_dynamic-update-slice_fusion.10
  918.1 4.8 constant_dynamic-update-slice_fusion.9
  922.9 4.4 constant_dynamic-update-slice_fusion.8
  927.3 4.7 constant_dynamic-update-slice_fusion.7
  932.0 4.7 constant_dynamic-update-slice_fusion.6
  936.7 4.7 constant_dynamic-update-slice_fusion.5
  941.4 4.7 constant_dynamic-update-slice_fusion.4
  946.1 4.8 constant_dynamic-update-slice_fusion.3
  950.9 4.7 constant_dynamic-update-slice_fusion.2
  955.6 4.7 constant_dynamic-update-slice_fusion.1
  960.3 4.6 constant_dynamic-update-slice_fusion
  964.9 15.9 %fusion.47 = f32[2,16,512]{2,1,0:T(8,128)} fusion(bf16[1024,128,256]{2,0,1:T(8,128)(2,1)} %constant_dynamic-update-slice_fusion, s32[]{:T(128)S(6)} %select_n.24, bf16[2,16,128,256]{3,2,1,0:T(8,128)(2,1)S(1)} %copy-done.1), kind=kOutput, calls=%fused_computation.31 | convolution fusion | flops 1073741824 | bytes 35717124 | tf_op jit(solution)/shard_map/dot_general | solution.py:34
  980.8 0.0 reduce-scatter.9.cloned.1.call-start
  980.9 16.3 %fusion.42 = f32[2,16,512]{2,1,0:T(8,128)} fusion(bf16[1024,128,256]{2,0,1:T(8,128)(2,1)} %constant_dynamic-update-slice_fusion, s32[]{:T(128)S(6)} %select_n.24, bf16[2,16,128,256]{3,2,1,0:T(8,128)(2,1)} %convert_bitcast_fusion.1), kind=kOutput, calls=%fused_computation.30 | convolution fusion | flops 1073741824 | bytes 35717124 | tf_op jit(solution)/shard_map/dot_general | solution.py:34
  997.2 0.0 reduce-scatter.7.cloned.1.call-start
  997.3 16.4 %fusion.37 = f32[2,16,512]{2,1,0:T(8,128)} fusion(bf16[1024,128,256]{2,0,1:T(8,128)(2,1)} %constant_dynamic-update-slice_fusion, s32[]{:T(128)S(6)} %select_n.24, bf16[2,16,128,256]{3,2,1,0:T(8,128)(2,1)} %convert_bitcast_fusion.2), kind=kOutput, calls=%fused_computation.29 | convolution fusion | flops 1073741824 | bytes 35717124 | tf_op jit(solution)/shard_map/dot_general | solution.py:34
  1013.7 0.0 reduce-scatter.5.cloned.1.call-start
  1013.7 15.9 %fusion.32 = f32[2,16,512]{2,1,0:T(8,128)} fusion(bf16[1024,128,256]{2,0,1:T(8,128)(2,1)} %constant_dynamic-update-slice_fusion, s32[]{:T(128)S(6)} %select_n.24, bf16[2,16,128,256]{3,2,1,0:T(8,128)(2,1)S(1)} %convert_bitcast_fusion.3), kind=kOutput, calls=%fused_computation.28 | convolution fusion | flops 1073741824 | bytes 35717124 | tf_op jit(solution)/shard_map/dot_general | solution.py:34
  1029.7 0.1 broadcast_subtract_fusion
  1029.8 12.7 %reduce-scatter.7.cloned.1.call-done = f32[2,16,128]{2,1,0:T(8,128)} async-done(((f32[2,16,512]{2,1,0:T(8,128)}), f32[2,16,128]{2,1,0:T(8,128)}) %reduce-scatter.7.cloned.1.call-update) | async-done | bytes 16400 | tf_op jit(solution)/shard_map/reduce_scatter | solution.py:39
  1042.4 22.0 %reduce-scatter.5.cloned.1.call-done = f32[2,16,128]{2,1,0:T(8,128)} async-done(((f32[2,16,512]{2,1,0:T(8,128)}), f32[2,16,128]{2,1,0:T(8,128)}) %reduce-scatter.5.cloned.1.call-update) | async-done | bytes 16400 | tf_op jit(solution)/shard_map/reduce_scatter | solution.py:39
  1064.5 1.5 maximum_divide_fusion
  (37 shorter events, 0.3 us)
Async XLA Ops:
  6.5 865.5 %all-gather.11.cloned.1.call-start = ((), (), s32[]{:S(2)}) async-start(), calls=%async_computation.11 | async-start | bytes 4718592 | tf_op jit(solution)/shard_map/all_gather | solution.py:26
  9.5 774.8 %copy-start.4 = (f32[512]{0:T(512)S(1)}, f32[512]{0:T(512)}, u32[]{:S(2)}) copy-start(f32[512]{0:T(512)} %param.11) | copy-start | bytes 6148
  9.5 774.9 %copy-start.2 = (s32[2,2]{1,0:T(2,128)S(1)}, s32[2,2]{1,0:T(2,128)}, u32[]{:S(2)}) copy-start(s32[2,2]{1,0:T(2,128)} %param.9) | copy-start | bytes 52
  9.5 775.1 %copy-start.3 = (f32[128]{0:T(128)S(1)}, f32[128]{0:T(128)}, u32[]{:S(2)}) copy-start(f32[128]{0:T(128)} %param.10) | copy-start | bytes 1540
  9.5 867.4 %all-gather.9.cloned.1.call-start = ((), (), s32[]{:S(2)}) async-start(), calls=%async_computation.9 | async-start | bytes 4718592 | tf_op jit(solution)/shard_map/all_gather | solution.py:26
  14.1 147.4 %collective-permute-start = (bf16[64,128,256]{2,0,1:T(8,128)(2,1)S(1)}, bf16[64,128,256]{2,0,1:T(8,128)(2,1)}, u32[]{:S(2)}, u32[]{:S(2)}) collective-permute-start(bf16[64,128,256]{2,0,1:T(8,128)(2,1)S(1)} %copy.27), channel_id=1, source_target_pairs={{0,4},{4,8},{8,12},{12,16},{16,20},{20,24},{24,28},{28,0},{1,5},{5... | collective-permute-start | bytes 12582920 | tf_op jit(solution)/shard_map/ppermute | solution.py:10
  161.5 145.4 %collective-permute-start.1 = (bf16[64,128,256]{2,0,1:T(8,128)(2,1)}, bf16[64,128,256]{2,0,1:T(8,128)(2,1)}, u32[]{:S(2)}, u32[]{:S(2)}) collective-permute-start(bf16[64,128,256]{2,0,1:T(8,128)(2,1)} %collective-permute-done), channel_id=1, source_target_pairs={{0,4},{4,8},{8,12},{12,16},{16,20},{20,24},{24,28},{28,0},{1,5},{5... | collective-permute-start | bytes 12582920 | tf_op jit(solution)/shard_map/ppermute | solution.py:10
  161.5 720.2 %all-gather.7.cloned.1.call-start = ((), (), s32[]{:S(2)}) async-start(), calls=%async_computation.7 | async-start | bytes 4718592 | tf_op jit(solution)/shard_map/all_gather | solution.py:26
  306.9 93.8 %collective-permute-start.2 = (bf16[64,128,256]{2,0,1:T(8,128)(2,1)}, bf16[64,128,256]{2,0,1:T(8,128)(2,1)}, u32[]{:S(2)}, u32[]{:S(2)}) collective-permute-start(bf16[64,128,256]{2,0,1:T(8,128)(2,1)} %collective-permute-done.1), channel_id=1, source_target_pairs={{0,4},{4,8},{8,12},{12,16},{16,20},{20,24},{24,28},{28,0},{1,5},{5... | collective-permute-start | bytes 12582920 | tf_op jit(solution)/shard_map/ppermute | solution.py:10
  400.7 143.6 %collective-permute-start.3 = (bf16[64,128,256]{2,0,1:T(8,128)(2,1)}, bf16[64,128,256]{2,0,1:T(8,128)(2,1)}, u32[]{:S(2)}, u32[]{:S(2)}) collective-permute-start(bf16[64,128,256]{2,0,1:T(8,128)(2,1)} %collective-permute-done.2), channel_id=1, source_target_pairs={{0,4},{4,8},{8,12},{12,16},{16,20},{20,24},{24,28},{28,0},{1,5},{5... | collective-permute-start | bytes 12582920 | tf_op jit(solution)/shard_map/ppermute | solution.py:10
  400.8 485.7 %all-gather.5.cloned.1.call-start = ((), (), s32[]{:S(2)}) async-start(), calls=%async_computation.5 | async-start | bytes 4718592 | tf_op jit(solution)/shard_map/all_gather | solution.py:26
  544.3 92.0 %collective-permute-start.4 = (bf16[64,128,256]{2,0,1:T(8,128)(2,1)}, bf16[64,128,256]{2,0,1:T(8,128)(2,1)}, u32[]{:S(2)}, u32[]{:S(2)}) collective-permute-start(bf16[64,128,256]{2,0,1:T(8,128)(2,1)} %collective-permute-done.3), channel_id=1, source_target_pairs={{0,4},{4,8},{8,12},{12,16},{16,20},{20,24},{24,28},{28,0},{1,5},{5... | collective-permute-start | bytes 12582920 | tf_op jit(solution)/shard_map/ppermute | solution.py:10
  636.3 141.7 %collective-permute-start.5 = (bf16[64,128,256]{2,0,1:T(8,128)(2,1)}, bf16[64,128,256]{2,0,1:T(8,128)(2,1)}, u32[]{:S(2)}, u32[]{:S(2)}) collective-permute-start(bf16[64,128,256]{2,0,1:T(8,128)(2,1)} %collective-permute-done.4), channel_id=1, source_target_pairs={{0,4},{4,8},{8,12},{12,16},{16,20},{20,24},{24,28},{28,0},{1,5},{5... | collective-permute-start | bytes 12582920 | tf_op jit(solution)/shard_map/ppermute | solution.py:10
  778.0 111.9 %collective-permute-start.6 = (bf16[64,128,256]{2,0,1:T(8,128)(2,1)}, bf16[64,128,256]{2,0,1:T(8,128)(2,1)}, u32[]{:S(2)}, u32[]{:S(2)}) collective-permute-start(bf16[64,128,256]{2,0,1:T(8,128)(2,1)} %collective-permute-done.5), channel_id=1, source_target_pairs={{0,4},{4,8},{8,12},{12,16},{16,20},{20,24},{24,28},{28,0},{1,5},{5... | collective-permute-start | bytes 12582920 | tf_op jit(solution)/shard_map/ppermute | solution.py:10
  778.1 93.9 %all-to-all-start = ((bf16[16,64,128]{2,1,0:T(8,128)(2,1)}), bf16[16,64,128]{2,1,0:T(8,128)(2,1)S(1)}, u32[]{:S(2)}, u32[]{:S(2)}) async-start(bf16[16,64,128]{2,1,0:T(8,128)(2,1)} %param.6), calls=%async_computation | async-start | bytes 524288 | tf_op jit(solution)/shard_map/all_to_all | solution.py:19
  784.0 245.7 %reduce-scatter.11.cloned.1.call-start = ((), (), s32[]{:S(2)}) async-start(), calls=%async_computation.12 | async-start | bytes 81920 | tf_op jit(solution)/shard_map/reduce_scatter | solution.py:39
  918.1 4.8 copy-start
  960.3 4.6 copy-start.1
  980.8 49.0 %reduce-scatter.9.cloned.1.call-start = ((), (), s32[]{:S(2)}) async-start(), calls=%async_computation.10 | async-start | bytes 81920 | tf_op jit(solution)/shard_map/reduce_scatter | solution.py:39
  997.2 45.2 %reduce-scatter.7.cloned.1.call-start = ((), (), s32[]{:S(2)}) async-start(), calls=%async_computation.8 | async-start | bytes 81920 | tf_op jit(solution)/shard_map/reduce_scatter | solution.py:39
  1013.7 16.0 %slice-start = ((f32[512]{0:T(512)}), f32[64]{0:T(128)S(1)}, s32[]{:S(2)}) async-start(f32[512]{0:T(512)} %param.11), calls=%async_computation.13 | async-start | bytes 1024 | tf_op jit(solution)/shard_map/slice | solution.py:54
  1013.7 50.8 %reduce-scatter.5.cloned.1.call-start = ((), (), s32[]{:S(2)}) async-start(), calls=%async_computation.6 | async-start | bytes 81920 | tf_op jit(solution)/shard_map/reduce_scatter | solution.py:39
Sparse Core Ops, SparseCore 0:
  9.6 115.5 all-gather.10
  161.6 114.3 all-gather.8
  400.9 113.9 all-gather.6
  636.5 113.5 all-gather.4
  980.9 17.5 reduce-scatter.10
  1001.0 19.4 reduce-scatter.8
  1022.9 19.5 reduce-scatter.6
  1045.0 19.4 reduce-scatter.4
